TPU v7x, 32 devices: a whole 2x2x4 slice. The times are simulated.
32 devices in a mesh: dp: 16 (over z, y, core), head: 2 (over x).
Axes of the slice: x: 2, y: 2, z: 4, core: 2. Of those that a mesh axis runs over, the one named last changes fastest.
Arguments:
- layer_input: bfloat16 [16, 256, 768], P('dp', 'head'), may hold values from -6 to 6
- pair_input: bfloat16 [16, 256, 256, 256], P('dp', 'head'), may hold values from -6 to 6
- time_cond: float32 [16, 256], P('dp'), may hold values from -6 to 6
- chain_lengths: int32 [16], P('dp'), may hold values from 128 to 256, as said below
- residue_mask: int32 [16, 256], P('dp'), may hold values from 0 to 1, as said below
- mod_weight: bfloat16 [256, 4608], replicated, may hold values from -0.375 to 0.375
- mod_bias: float32 [4608], replicated, may hold values from -3 to 3
- qkv_weight: bfloat16 [768, 3, 768], P(None, None, 'head'), may hold values from -0.21875 to 0.21875
- pair_gain: float32 [256], replicated, may hold values from 0.25 to 1.75
- pair_weight: bfloat16 [256, 12], replicated, may hold values from -0.375 to 0.375
- out_weight: bfloat16 [768, 768], P('head'), may hold values from -0.625 to 0.625
- out_bias: float32 [768], replicated, may hold values from -3 to 3
- gate_up_weight: bfloat16 [768, 2, 3072], P(None, None, 'head'), may hold values from -0.21875 to 0.21875
- down_weight: bfloat16 [3072, 768], P('head'), may hold values from -0.21875 to 0.21875
- output_grad: bfloat16 [16, 256, 768], P('dp', 'head'), may hold values from -6 to 6
Outputs:
- layer_output: bfloat16 [16, 256, 768], P('dp', 'head')
- input_grad: float32 [16, 256, 768], P('dp', 'head')
- pair_grad: bfloat16 [16, 256, 256, 256], P('dp', 'head')
- cond_grad: float32 [16, 256], P('dp')
- mod_weight_grad: float32 [256, 4608], replicated
- mod_bias_grad: float32 [4608], replicated
- qkv_weight_grad: float32 [768, 3, 768], P('dp', None, 'head')
- pair_gain_grad: float32 [256], replicated
- pair_weight_grad: float32 [256, 12], replicated
- out_weight_grad: float32 [768, 768], P('head', 'dp')
- out_bias_grad: float32 [768], replicated
- gate_up_grad: float32 [768, 2, 3072], P('dp', None, 'head')
- down_grad: float32 [3072, 768], P('head', 'dp')
Inputs may be any that keep to these rules, and one draw needn't show every extreme that they name: `chain_lengths`: each chain has 128 to 256 residues in use; the first chain has all 256. `residue_mask`: the first residue of every chain is resolved.
All inputs are finite; a program needn't handle non-finite values.
Results may differ from a plain program's by a relative error of at most 0.014.
The roundings to bfloat16 on the way count: a program that leaves them out, or rounds other values in their place, can miss the bound.
Values may be sent and summed in bfloat16 or wider, within the bound.
No kernel may reach another device: no remote copies, remote signals or barrier semaphores. Data moves between devices by JAX's collectives and lax.ppermute only.
A program may use at most 256 MiB of HBM per device.

v0:
```python
import jax
import jax.numpy as jnp
from jax import lax
from jax.sharding import PartitionSpec as P

DH = 64


epsilon = 1e-05
masked_score = -1000000000.0
precise = lax.Precision.HIGHEST


def layer_norm(values):
    centred = values - jnp.mean(values, axis=-1, keepdims=True)
    inv_std = lax.rsqrt(jnp.mean(centred * centred, axis=-1, keepdims=True) + epsilon)
    return (centred * inv_std, inv_std)


def norm_back(normed, inv_std, grad):
    mean_grad = jnp.mean(grad, axis=-1, keepdims=True)
    mean_proj = jnp.mean(grad * normed, axis=-1, keepdims=True)
    return inv_std * (grad - mean_grad - normed * mean_proj)


def silu_slope(values):
    sigma = jax.nn.sigmoid(values)
    return sigma * (1.0 + values * (1.0 - sigma))


def head_split(values):
    return values.reshape(values.shape[:-1] + (values.shape[-1] // DH, DH))


def project_rows(rows, qkv_weight):
    return jnp.einsum("cld,dtf->tclf", rows, qkv_weight, preferred_element_type=jnp.float32).astype(
        jnp.bfloat16
    )


def attn_scores(queries, keys, biases, valid):
    scores = jnp.einsum("cqhe,ckhe->chqk", queries, keys, preferred_element_type=jnp.float32)
    scores = scores * DH ** (-0.5) + biases.astype(jnp.float32)
    return jnp.where(valid[:, None, None, :], scores, masked_score)


def attend_forward(projected, biases, valid):
    queries = head_split(projected[0])
    keys = head_split(projected[1])
    values = head_split(projected[2])
    scores = attn_scores(queries, keys, biases, valid)
    row_max = jnp.max(scores, axis=-1, keepdims=True)
    exp_scores = jnp.exp(scores - row_max)
    row_total = jnp.sum(exp_scores, axis=-1, keepdims=True)
    attn_probs = (exp_scores / row_total).astype(jnp.bfloat16)
    mixed = jnp.einsum("chqk,ckhe->cqhe", attn_probs, values, preferred_element_type=jnp.float32)
    mixed = mixed.reshape(mixed.shape[:2] + (-1,)).astype(jnp.bfloat16)
    return (mixed, row_max + jnp.log(row_total))


def transition_forward(rows, gate_up_weight):
    gate_up = jnp.einsum("cld,dtf->tclf", rows, gate_up_weight, preferred_element_type=jnp.float32)
    hidden = (jax.nn.silu(gate_up[0]) * gate_up[1]).astype(jnp.bfloat16)
    return (gate_up, hidden)


def shards(
    layer_input,
    pair_input,
    time_cond,
    chain_lengths,
    residue_mask,
    mod_weight,
    mod_bias,
    qkv_weight,
    pair_gain,
    pair_weight,
    out_weight,
    out_bias,
    gate_up_weight,
    down_weight,
    output_grad,
):
    chains = layer_input.shape[0]
    width = layer_input.shape[2]
    length = residue_mask.shape[1]
    positions = jnp.arange(length, dtype=jnp.int32)
    valid = (positions[None, :] < chain_lengths[:, None]) & (
        (residue_mask == 1) | (positions[None, :] == 0)
    )
    silu_cond = jax.nn.silu(time_cond).astype(jnp.bfloat16)
    modulation = jnp.dot(silu_cond, mod_weight, preferred_element_type=jnp.float32) + mod_bias
    scale_a, shift_a, gate_a, scale_t, shift_t, gate_t = [
        modulation[:, None, section * width : (section + 1) * width] for section in range(6)
    ]
    residues = layer_input.astype(jnp.float32)
    norm_in, inv_in = layer_norm(residues)
    normed_a = (norm_in * (1.0 + scale_a) + shift_a).astype(jnp.bfloat16)
    rows_a = lax.all_gather(normed_a, "head", axis=1, tiled=True)
    projected = project_rows(rows_a, qkv_weight)
    pair_norm, pair_inv = layer_norm(pair_input.astype(jnp.float32))
    pair_normed = (pair_norm * pair_gain).astype(jnp.bfloat16)
    bias_rows = jnp.einsum(
        "cqkp,ph->chqk", pair_normed, pair_weight, preferred_element_type=jnp.float32
    ).astype(jnp.bfloat16)
    biases = lax.all_to_all(bias_rows, "head", split_axis=1, concat_axis=2, tiled=True)
    mixed, log_total = attend_forward(projected, biases, valid)
    attn_part = jnp.einsum("clf,fd->cld", mixed, out_weight, preferred_element_type=jnp.float32)
    attn_branch = lax.psum_scatter(attn_part, "head", scatter_dimension=1, tiled=True) + out_bias
    sig_a = jax.nn.sigmoid(gate_a)
    middle = residues + sig_a * attn_branch
    norm_mid, inv_mid = layer_norm(middle)
    normed_t = (norm_mid * (1.0 + scale_t) + shift_t).astype(jnp.bfloat16)
    rows_t = lax.all_gather(normed_t, "head", axis=1, tiled=True)
    gate_up, hidden = transition_forward(rows_t, gate_up_weight)
    ffn_part = jnp.einsum("clf,fd->cld", hidden, down_weight, preferred_element_type=jnp.float32)
    ffn_branch = lax.psum_scatter(
        ffn_part.astype(jnp.bfloat16), "head", scatter_dimension=1, tiled=True
    ).astype(jnp.float32)
    sig_t = jax.nn.sigmoid(gate_t)
    layer_output = (middle + sig_t * ffn_branch).astype(jnp.bfloat16)
    grad_out = output_grad.astype(jnp.float32)
    d_ffn = (grad_out * sig_t).astype(jnp.bfloat16)
    d_gate_t = jnp.sum(grad_out * ffn_branch * sig_t * (1.0 - sig_t), axis=1)
    ffn_grads, ffn_rows_used = (
        lax.all_gather(d_ffn, "head", axis=1, tiled=True),
        lax.all_gather(normed_t, "head", axis=1, tiled=True),
    )
    gate_used, hidden_used = transition_forward(ffn_rows_used, gate_up_weight)
    down_grad = jnp.einsum(
        "clf,cld->fd", hidden_used, ffn_grads, preferred_element_type=jnp.float32
    )
    d_hidden = jnp.einsum("cld,fd->clf", ffn_grads, down_weight, preferred_element_type=jnp.float32)
    d_gate = d_hidden * gate_used[1] * silu_slope(gate_used[0])
    d_up = d_hidden * jax.nn.silu(gate_used[0])
    d_gate_up = jnp.stack([d_gate, d_up]).astype(jnp.bfloat16)
    gate_up_grad = jnp.einsum(
        "cld,tclf->dtf", ffn_rows_used, d_gate_up, preferred_element_type=jnp.float32
    )
    ffn_in_part = jnp.einsum(
        "tclf,dtf->cld", d_gate_up, gate_up_weight, preferred_element_type=jnp.float32
    )
    d_normed_t = lax.psum_scatter(ffn_in_part, "head", scatter_dimension=1, tiled=True)
    d_middle = grad_out + norm_back(norm_mid, inv_mid, d_normed_t * (1.0 + scale_t))
    d_scale_t = jnp.sum(d_normed_t * norm_mid, axis=1)
    d_shift_t = jnp.sum(d_normed_t, axis=1)
    d_attn = d_middle * sig_a
    d_gate_a = jnp.sum(d_middle * attn_branch * sig_a * (1.0 - sig_a), axis=1)
    d_out_bias = jnp.sum(d_attn, axis=(0, 1))
    d_attn_low = d_attn.astype(jnp.bfloat16)
    attn_grads, rows_a_used = (
        lax.all_gather(d_attn_low, "head", axis=1, tiled=True),
        lax.all_gather(normed_a, "head", axis=1, tiled=True),
    )
    projected_used = project_rows(rows_a_used, qkv_weight)
    mixed_used = attend_forward(projected_used, biases, valid)[0]
    out_weight_grad = jnp.einsum(
        "clf,cld->fd", mixed_used, attn_grads, preferred_element_type=jnp.float32
    )
    d_mixed = head_split(
        jnp.einsum(
            "cld,fd->clf", attn_grads, out_weight, preferred_element_type=jnp.float32
        ).astype(jnp.bfloat16)
    )
    queries = head_split(projected_used[0])
    keys = head_split(projected_used[1])
    values = head_split(projected_used[2])
    scores = attn_scores(queries, keys, biases, valid)
    attn_probs = jnp.exp(scores - log_total)
    probs_low = attn_probs.astype(jnp.bfloat16)
    d_values = jnp.einsum("chqk,cqhe->ckhe", probs_low, d_mixed, preferred_element_type=jnp.float32)
    d_probs = jnp.einsum("cqhe,ckhe->chqk", d_mixed, values, preferred_element_type=jnp.float32)
    d_scores = (
        attn_probs * (d_probs - jnp.sum(d_probs * attn_probs, axis=-1, keepdims=True))
    ).astype(jnp.bfloat16)
    d_queries = jnp.einsum(
        "chqk,ckhe->cqhe", d_scores, keys, preferred_element_type=jnp.float32
    ) * DH ** (-0.5)
    d_keys = jnp.einsum(
        "chqk,cqhe->ckhe", d_scores, queries, preferred_element_type=jnp.float32
    ) * DH ** (-0.5)
    d_qkv = (
        jnp.stack([d_queries, d_keys, d_values]).reshape(3, chains, length, -1).astype(jnp.bfloat16)
    )
    qkv_grad = jnp.einsum("cld,tclf->dtf", rows_a_used, d_qkv, preferred_element_type=jnp.float32)
    attn_in_part = jnp.einsum(
        "tclf,dtf->cld", d_qkv, qkv_weight, preferred_element_type=jnp.float32
    )
    d_normed_a = lax.psum_scatter(
        attn_in_part.astype(jnp.bfloat16), "head", scatter_dimension=1, tiled=True
    ).astype(jnp.float32)
    d_bias_rows = lax.all_to_all(d_scores, "head", split_axis=2, concat_axis=1, tiled=True)
    pair_weight_grad = jnp.einsum(
        "cqkp,chqk->ph", pair_normed, d_bias_rows, preferred_element_type=jnp.float32
    )
    d_pair_normed = jnp.einsum(
        "chqk,ph->cqkp", d_bias_rows, pair_weight, preferred_element_type=jnp.float32
    )
    pair_gain_grad = jnp.sum(d_pair_normed * pair_norm, axis=(0, 1, 2))
    pair_grad = norm_back(pair_norm, pair_inv, d_pair_normed * pair_gain).astype(jnp.bfloat16)
    input_grad = d_middle + norm_back(norm_in, inv_in, d_normed_a * (1.0 + scale_a))
    d_scale_a = jnp.sum(d_normed_a * norm_in, axis=1)
    d_shift_a = jnp.sum(d_normed_a, axis=1)
    d_modulation = jnp.concatenate(
        [d_scale_a, d_shift_a, d_gate_a, d_scale_t, d_shift_t, d_gate_t], axis=-1
    )
    pair_weight_grad, pair_gain_grad, out_bias_grad = lax.psum(
        (pair_weight_grad, pair_gain_grad, d_out_bias), ("dp", "head")
    )
    mod_rows, cond_rows = (
        lax.all_gather(d_modulation, ("dp", "head"), axis=0, tiled=True),
        lax.all_gather(time_cond, ("dp", "head"), axis=0, tiled=True),
    )
    data_count = lax.axis_size("dp")
    head_count = lax.axis_size("head")
    mod_chain = jnp.sum(mod_rows.reshape(data_count, head_count, chains, -1), axis=1).reshape(
        data_count * chains, -1
    )
    cond_chain = cond_rows.reshape(data_count, head_count, chains, -1)[:, 0].reshape(
        data_count * chains, -1
    )
    cond_act = lax.optimization_barrier(jax.nn.silu(cond_chain).astype(jnp.bfloat16)).astype(
        jnp.float32
    )
    mod_weight_grad = jnp.dot(cond_act.T, mod_chain, precision=precise)
    mod_bias_grad = jnp.sum(mod_chain, axis=0)
    own_rows = lax.dynamic_slice_in_dim(mod_chain, lax.axis_index("dp") * chains, chains, 0)
    cond_grad = jnp.dot(own_rows, mod_weight.astype(jnp.float32).T, precision=precise) * silu_slope(
        time_cond
    )
    qkv_grad, out_weight_grad, gate_up_grad, down_grad = (
        lax.psum_scatter(qkv_grad, "dp", scatter_dimension=0, tiled=True),
        lax.psum_scatter(out_weight_grad, "dp", scatter_dimension=1, tiled=True),
        lax.psum_scatter(gate_up_grad, "dp", scatter_dimension=0, tiled=True),
        lax.psum_scatter(down_grad, "dp", scatter_dimension=1, tiled=True),
    )
    return (
        layer_output,
        input_grad,
        pair_grad,
        cond_grad,
        mod_weight_grad,
        mod_bias_grad,
        qkv_grad,
        pair_gain_grad,
        pair_weight_grad,
        out_weight_grad,
        out_bias_grad,
        gate_up_grad,
        down_grad,
    )


def solution(mesh):
    placed = (
        P("dp", "head", None),
        P("dp", "head", None, None),
        P("dp", None),
        P("dp"),
        P("dp", None),
        P(),
        P(),
        P(None, None, "head"),
        P(),
        P(),
        P("head", None),
        P(),
        P(None, None, "head"),
        P("head", None),
        P("dp", "head", None),
    )
    return jax.shard_map(
        shards,
        mesh=mesh,
        in_specs=placed,
        out_specs=(
            P("dp", "head", None),
            P("dp", "head", None),
            P("dp", "head", None, None),
            P("dp", None),
            P(),
            P(),
            P("dp", None, "head"),
            P(),
            P(),
            P("head", "dp"),
            P(),
            P("dp", None, "head"),
            P("head", "dp"),
        ),
        check_vma=False,
    )
```

profile of v0, /device:TPU:0, one launch (start us, length us, event | category | flops | bytes accessed | tf_op | source)
XLA Modules:
  0.0 530.2 jit_solution(12424743062882511665)
XLA Ops:
  7.2 22.6 %copy.109 = bf16[1,128,256,256]{2,3,1,0:T(8,128)(2,1)} copy(bf16[1,128,256,256]{3,2,1,0:T(8,128)(2,1)} %param.16) | data formatting | bytes 33554432 | tf_op args[1]
  29.8 6.9 %convert_reduce_fusion = f32[128,256]{1,0:T(8,128)S(1)} fusion(bf16[1,128,256,256]{2,3,1,0:T(8,128)(2,1)} %copy.109), kind=kLoop, calls=%fused_computation.1 | loop fusion | flops 16744448 | bytes 16908288 | tf_op jit(solution)/shard_map/reduce_sum | solution.py:15
  36.7 3.7 copy-done.2
  40.4 4.7 fusion.12
  45.2 5.2 fusion.37
  51.5 4.4 all-to-all-start
  59.5 13.0 %all_gather.20 = bf16[1,256,768]{2,1,0:T(8,128)(2,1)S(1)} all-gather(bf16[1,128,768]{2,1,0:T(8,128)(2,1)S(1)} %fusion.72), channel_id=1, replica_groups=mesh['dp'=16,'head'=2] {'head'}, dimensions={1}, use_global_device_ids=true | all-gather | bytes 589824 | tf_op jit(solution)/shard_map/all_gather | solution.py:99
  76.9 3.6 copy.113
  80.6 3.3 reshape.540
  89.3 6.8 %all_gather.22 = bf16[1,256,768]{2,1,0:T(8,128)(2,1)} all-gather(bf16[1,128,768]{2,1,0:T(8,128)(2,1)S(1)} %fusion.80), channel_id=1, replica_groups=mesh['dp'=16,'head'=2] {'head'}, dimensions={1}, use_global_device_ids=true | all-gather | bytes 589824 | tf_op jit(solution)/shard_map/all_gather | solution.py:126
  96.1 11.3 %reduce-scatter.9.cloned.1.call-done = f32[1,128,768]{2,1,0:T(8,128)} async-done(((f32[1,256,768]{2,1,0:T(8,128)}), f32[1,128,768]{2,1,0:T(8,128)}) %reduce-scatter.9.cloned.1.call-update) | async-done | bytes 393232 | tf_op jit(solution)/shard_map/reduce_scatter | solution.py:109
  109.7 7.3 %all_gather.21 = bf16[1,256,768]{2,1,0:T(8,128)(2,1)S(1)} all-gather(bf16[1,128,768]{2,1,0:T(8,128)(2,1)S(1)} %add_convert_fusion), channel_id=1, replica_groups=mesh['dp'=16,'head'=2] {'head'}, dimensions={1}, use_global_device_ids=true | all-gather | bytes 589824 | tf_op jit(solution)/shard_map/all_gather | solution.py:114
  117.0 3.9 fusion.18
  126.3 3.6 fusion.46
  130.0 13.8 %reduce-scatter.13.cloned.1.call-done = f32[1,128,768]{2,1,0:T(8,128)} async-done(((f32[1,256,768]{2,1,0:T(8,128)}), f32[1,128,768]{2,1,0:T(8,128)}) %reduce-scatter.13.cloned.1.call-update) | async-done | bytes 393232 | tf_op jit(solution)/shard_map/reduce_scatter | solution.py:143
  145.7 14.2 %reduce-scatter.11.cloned.1.call-done = bf16[1,128,768]{2,1,0:T(8,128)(2,1)} async-done(((bf16[1,256,768]{2,1,0:T(8,128)(2,1)}), bf16[1,128,768]{2,1,0:T(8,128)(2,1)}) %reduce-scatter.11.cloned.1.call-update) | async-done | bytes 196624 | tf_op jit(solution)/shard_map/reduce_scatter | solution.py:117
  162.9 7.3 %all_gather.23 = bf16[1,256,768]{2,1,0:T(8,128)(2,1)S(1)} all-gather(bf16[1,128,768]{2,1,0:T(8,128)(2,1)S(1)} %multiply_convert_fusion.4), channel_id=1, replica_groups=mesh['dp'=16,'head'=2] {'head'}, dimensions={1}, use_global_device_ids=true | all-gather | bytes 589824 | tf_op jit(solution)/shard_map/all_gather | solution.py:152
  180.7 6.2 %fusion.56 = f32[768,2,1536]{2,0,1:T(8,128)} fusion(bf16[1,256,1536]{2,1,0:T(8,128)(2,1)} %copy-done.18, bf16[1,256,1536]{2,1,0:T(8,128)(2,1)S(1)} %copy-done.17, bf16[1,256,768]{2,1,0:T(8,128)(2,1)S(1)} %copy-done.7), kind=kOutput, calls=%fused_computation.73 | convolution fusion | flops 1211105280 | bytes 11403264 | tf_op jit(solution)/shard_map/cld,tclf->dtf/dot_general | solution.py:137
  192.5 67.7 %all-gather.1 = f32[32,1,256]{2,1,0:T(1,128)S(1)} all-gather(f32[1,1,256]{2,1,0:T(1,128)S(1)} %bitcast.233), channel_id=1, replica_groups=mesh['dp'=16,'head'=2] {'dp','head'}, dimensions={0}, use_global_device_ids=true | all-gather | bytes 33792 | tf_op jit(solution)/shard_map/all_gather | solution.py:212
  261.9 3.6 all-to-all-start.1
  265.8 5.2 fusion.60
  271.1 5.4 %all-to-all-done.1 = bf16[1,6,256,256]{3,1,0,2:T(8,128)(2,1)S(1)} async-done(((bf16[1,6,256,256]{3,1,0,2:T(8,128)(2,1)}), bf16[1,6,256,256]{3,1,0,2:T(8,128)(2,1)S(1)}, u32[]{:S(2)}, u32[]{:S(2)}) %all-to-all-start.1) | async-done | bytes 786464 | tf_op jit(solution)/shard_map/all_to_all | solution.py:192
  276.8 21.5 %fusion.11 = (f32[256]{0:T(256)S(1)}, f32[128,256]{1,0:T(8,128)S(1)}, f32[128,256,256]{1,2,0:T(8,128)}) fusion(bf16[1,128,256,256]{2,3,1,0:T(8,128)(2,1)} %copy.109, f32[128,256]{1,0:T(8,128)S(1)} %copy-done.27, f32[128,256]{1,0:T(8,128)S(1)} %copy-done.15, f32[256]{0:T(256)S(1)} %copy-done.56, bf16[256,12]{0,1:T(8,128)(2,1)S(1)} %copy-done.60, ...), kind=kOutput, calls=%fused_computation.13 | convolution fusion | flops 268402432 | bytes 51519488 | tf_op jit(solution)/shard_map/chqk,ph->cqkp/dot_general | solution.py:196
  298.3 14.5 %multiply_reduce_fusion = f32[128,256]{1,0:T(8,128)S(1)} fusion(f32[128,256,256]{1,2,0:T(8,128)} %get-tuple-element.102, f32[256]{0:T(256)S(1)} %copy-done.56), kind=kLoop, calls=%fused_computation.15 | loop fusion | flops 16744448 | bytes 33686528 | tf_op jit(solution)/shard_map/reduce_sum | solution.py:21
  312.9 24.8 %fusion.10 = bf16[1,128,256,256]{2,3,1,0:T(8,128)(2,1)} fusion(bf16[1,128,256,256]{2,3,1,0:T(8,128)(2,1)} %copy.109, f32[128,256,256]{1,2,0:T(8,128)} %get-tuple-element.102, f32[128,256]{1,0:T(8,128)S(1)} %broadcast_multiply_fusion, f32[128,256]{1,0:T(8,128)S(1)} %broadcast_multiply_fusion.1, f32[256]{0:T(256)S(1)} %copy-done.56, ...), kind=kLoop, calls=%fused_computation.12 | loop fusion | flops 75497472 | bytes 67634176 | tf_op jit(solution)/shard_map/convert_element_type | solution.py:200
  337.7 22.4 %copy.132 = bf16[1,128,256,256]{3,2,1,0:T(8,128)(2,1)} copy(bf16[1,128,256,256]{2,3,1,0:T(8,128)(2,1)} %fusion.10) | data formatting | bytes 33554432
  360.1 9.1 %fusion.50 = f32[256,12]{0,1:T(8,128)S(1)} fusion(bf16[1,128,256,256]{2,3,1,0:T(8,128)(2,1)} %copy.109, f32[256]{0:T(256)S(1)} %copy-done.56, f32[128,256]{1,0:T(8,128)S(1)} %copy-done.27, f32[128,256]{1,0:T(8,128)S(1)} %copy-done.15, bf16[12,128,256]{2,1,0:T(8,128)(2,1)S(1)} %bitcast.229), kind=kOutput, calls=%fused_computation.68 | convolution fusion | flops 243269632 | bytes 17839104 | tf_op jit(solution)/shard_map/cqkp,chqk->ph/dot_general | solution.py:193
  369.2 37.4 %all-reduce = (f32[256]{0:T(256)}, f32[256,12]{0,1:T(8,128)}, f32[768]{0:T(1024)}) all-reduce(f32[256]{0:T(256)S(1)} %get-tuple-element.65, f32[256,12]{0,1:T(8,128)S(1)} %fusion.50, f32[768]{0:T(1024)S(1)} %copy-done.44), channel_id=1, replica_groups=mesh['dp'=16,'head'=2] {'dp','head'}, use_global_device_ids=true, to_apply=%region_29.30 | all-reduce | flops 4096 | bytes 32768 | tf_op jit(solution)/shard_map/psum | solution.py:207
  408.0 71.3 %all-gather = f32[32,1,4608]{2,1,0:T(1,128)S(1)} all-gather(f32[1,1,4608]{2,1,0:T(1,128)S(1)} %bitcast.232), channel_id=1, replica_groups=mesh['dp'=16,'head'=2] {'dp','head'}, dimensions={0}, use_global_device_ids=true | all-gather | bytes 608256 | tf_op jit(solution)/shard_map/all_gather | solution.py:211
  482.9 4.3 convolution_multiply_fusion.2
  487.3 4.2 fusion.126
  493.8 29.1 %reduce-scatter.23.cloned.1.call-done = f32[1536,48]{0,1:T(8,128)} async-done(((f32[1536,768]{0,1:T(8,128)}), f32[1536,48]{0,1:T(8,128)}) %reduce-scatter.23.cloned.1.call-update) | async-done | bytes 294928 | tf_op jit(solution)/shard_map/reduce_scatter | solution.py:235
  (220 shorter events, 51.5 us)
Async XLA Ops:
  7.2 113.7 %copy-start = (bf16[1536,768]{1,0:T(8,128)(2,1)S(1)}, bf16[1536,768]{1,0:T(8,128)(2,1)}, u32[]{:S(2)}) copy-start(bf16[1536,768]{1,0:T(8,128)(2,1)} %param.28) | copy-start | bytes 7077892
  51.5 22.9 %all-to-all-start = ((bf16[1,12,128,256]{3,2,0,1:T(8,128)(2,1)}), bf16[1,12,128,256]{3,2,0,1:T(8,128)(2,1)}, u32[]{:S(2)}, u32[]{:S(2)}) async-start(bf16[1,12,128,256]{3,2,0,1:T(8,128)(2,1)} %copy.111), calls=%async_computation | async-start | bytes 1572864 | tf_op jit(solution)/shard_map/all_to_all | solution.py:106
  56.0 51.4 %reduce-scatter.9.cloned.1.call-start = ((), (), s32[]{:S(2)}) async-start(), calls=%async_computation.10 | async-start | bytes 1179648 | tf_op jit(solution)/shard_map/reduce_scatter | solution.py:109
  56.0 16.4 %copy-start.58 = (bf16[768,3,384]{2,0,1:T(8,128)(2,1)S(1)}, bf16[768,3,384]{2,0,1:T(8,128)(2,1)}, u32[]{:S(2)}) copy-start(bf16[768,3,384]{2,0,1:T(8,128)(2,1)} %param.22) | copy-start | bytes 5308420
  56.2 17.0 %copy-start.47 = (f32[128]{0:T(128)}, f32[128]{0:T(128)S(1)}, u32[]{:S(2)}) copy-start(f32[128]{0:T(128)S(1)} %broadcast_multiply_fusion.8) | copy-start | bytes 1540
  56.4 16.8 %copy-start.51 = (f32[128]{0:T(128)}, f32[128]{0:T(128)S(1)}, u32[]{:S(2)}) copy-start(f32[128]{0:T(128)S(1)} %add_rsqrt_fusion.2) | copy-start | bytes 1540
  87.2 21.5 %copy-start.19 = (bf16[6,64,256]{2,1,0:T(8,128)(2,1)}, bf16[6,64,256]{2,1,0:T(8,128)(2,1)S(1)}, u32[]{:S(2)}) copy-start(bf16[6,64,256]{2,1,0:T(8,128)(2,1)S(1)} %convolution_convert_fusion.4) | copy-start | bytes 589828
  87.9 19.5 %copy-start.39 = (f32[768]{0:T(1024)S(1)}, f32[768]{0:T(1024)}, u32[]{:S(2)}) copy-start(f32[768]{0:T(1024)} %param.26) | copy-start | bytes 9220
  87.9 20.9 %copy-start.32 = (f32[768]{0:T(1024)S(1)}, f32[768]{0:T(1024)}, u32[]{:S(2)}) copy-start(f32[768]{0:T(1024)} %get-tuple-element.81) | copy-start | bytes 9220
  89.2 54.6 %reduce-scatter.13.cloned.1.call-start = ((), (), s32[]{:S(2)}) async-start(), calls=%async_computation.12 | async-start | bytes 1179648 | tf_op jit(solution)/shard_map/reduce_scatter | solution.py:143
  108.6 12.3 %copy-start.49 = (f32[128]{0:T(128)}, f32[128]{0:T(128)S(1)}, u32[]{:S(2)}) copy-start(f32[128]{0:T(128)S(1)} %broadcast_multiply_fusion.7) | copy-start | bytes 1540
  126.2 17.7 %copy-start.33 = (f32[768]{0:T(1024)S(1)}, f32[768]{0:T(1024)}, u32[]{:S(2)}) copy-start(f32[768]{0:T(1024)} %get-tuple-element.81) | copy-start | bytes 9220
  126.2 17.7 %copy-start.50 = (f32[128]{0:T(128)S(1)}, f32[128]{0:T(128)}, u32[]{:S(2)}) copy-start(f32[128]{0:T(128)} %copy-done.49) | copy-start | bytes 1540
  126.2 17.6 %copy-start.54 = (f32[128]{0:T(128)S(1)}, f32[128]{0:T(128)}, u32[]{:S(2)}) copy-start(f32[128]{0:T(128)} %copy-done.53) | copy-start | bytes 1540
  126.2 33.7 %reduce-scatter.11.cloned.1.call-start = ((), (), s32[]{:S(2)}) async-start(), calls=%async_computation.11 | async-start | bytes 589824 | tf_op jit(solution)/shard_map/reduce_scatter | solution.py:117
  129.9 40.3 %copy-start.9 = (bf16[384,768]{1,0:T(8,128)(2,1)S(1)}, bf16[384,768]{1,0:T(8,128)(2,1)}, u32[]{:S(2)}) copy-start(bf16[384,768]{1,0:T(8,128)(2,1)} %param.25) | copy-start | bytes 1769476
  129.9 276.7 %reduce-scatter.15.cloned.1.call-start = ((), (), s32[]{:S(2)}) async-start(), calls=%async_computation.13 | async-start | bytes 589824 | tf_op jit(solution)/shard_map/reduce_scatter | solution.py:189
  159.9 12.4 %copy-start.4 = (f32[6,256,256]{1,2,0:T(8,128)S(1)}, f32[6,256,256]{1,2,0:T(8,128)}, u32[]{:S(2)}) copy-start(f32[6,256,256]{1,2,0:T(8,128)} %copy-done.3) | copy-start | bytes 4718596
  180.6 310.9 %reduce-scatter.21.cloned.1.call-start = ((), (), s32[]{:S(2)}) async-start(), calls=%async_computation.16 | async-start | bytes 10027008 | tf_op jit(solution)/shard_map/reduce_scatter | solution.py:234
  186.9 306.9 %reduce-scatter.19.cloned.1.call-start = ((), (), s32[]{:S(2)}) async-start(), calls=%async_computation.15 | async-start | bytes 1253376 | tf_op jit(solution)/shard_map/reduce_scatter | solution.py:233
  189.3 304.6 %reduce-scatter.17.cloned.1.call-start = ((), (), s32[]{:S(2)}) async-start(), calls=%async_computation.14 | async-start | bytes 3760128 | tf_op jit(solution)/shard_map/reduce_scatter | solution.py:232
  191.8 73.9 %copy-start.29 = (bf16[1,256,768]{2,1,0:T(8,128)(2,1)S(1)}, bf16[1,256,768]{2,1,0:T(8,128)(2,1)}, u32[]{:S(2)}) copy-start(bf16[1,256,768]{2,1,0:T(8,128)(2,1)} %all_gather.22) | copy-start | bytes 1179652
  261.9 14.6 %all-to-all-start.1 = ((bf16[1,6,256,256]{3,1,0,2:T(8,128)(2,1)}), bf16[1,6,256,256]{3,1,0,2:T(8,128)(2,1)S(1)}, u32[]{:S(2)}, u32[]{:S(2)}) async-start(bf16[1,6,256,256]{3,1,0,2:T(8,128)(2,1)} %copy.124), calls=%async_computation.5 | async-start | bytes 2097152 | tf_op jit(solution)/shard_map/all_to_all | solution.py:192
  265.5 257.4 %reduce-scatter.23.cloned.1.call-start = ((), (), s32[]{:S(2)}) async-start(), calls=%async_computation.17 | async-start | bytes 5013504 | tf_op jit(solution)/shard_map/reduce_scatter | solution.py:235
  360.1 46.5 %copy-start.48 = (f32[128]{0:T(128)S(1)}, f32[128]{0:T(128)}, u32[]{:S(2)}) copy-start(f32[128]{0:T(128)} %copy-done.47) | copy-start | bytes 1540
  360.1 46.5 %copy-start.52 = (f32[128]{0:T(128)S(1)}, f32[128]{0:T(128)}, u32[]{:S(2)}) copy-start(f32[128]{0:T(128)} %copy-done.51) | copy-start | bytes 1540
  360.1 47.8 %copy-start.43 = (f32[768]{0:T(1024)S(1)}, f32[768]{0:T(1024)}, u32[]{:S(2)}) copy-start(f32[768]{0:T(1024)} %get-tuple-element.73) | copy-start | bytes 9220
  360.1 47.8 %copy-start.41 = (f32[768]{0:T(1024)S(1)}, f32[768]{0:T(1024)}, u32[]{:S(2)}) copy-start(f32[768]{0:T(1024)} %get-tuple-element.67) | copy-start | bytes 9220
  360.1 47.8 %copy-start.40 = (f32[768]{0:T(1024)S(1)}, f32[768]{0:T(1024)}, u32[]{:S(2)}) copy-start(f32[768]{0:T(1024)} %get-tuple-element.76) | copy-start | bytes 9220
  360.1 47.9 %copy-start.42 = (f32[768]{0:T(1024)S(1)}, f32[768]{0:T(1024)}, u32[]{:S(2)}) copy-start(f32[768]{0:T(1024)} %get-tuple-element.97) | copy-start | bytes 9220
  406.6 75.4 %copy-start.22 = (bf16[1,128,768]{2,1,0:T(8,128)(2,1)S(1)}, bf16[1,128,768]{2,1,0:T(8,128)(2,1)}, u32[]{:S(2)}) copy-start(bf16[1,128,768]{2,1,0:T(8,128)(2,1)} %reduce-scatter.15.cloned.1.call-done) | copy-start | bytes 589828
  482.9 40.0 %copy-start.1 = (bf16[1536,768]{1,0:T(8,128)(2,1)S(1)}, bf16[1536,768]{1,0:T(8,128)(2,1)}, u32[]{:S(2)}) copy-start(bf16[1536,768]{1,0:T(8,128)(2,1)} %param.28) | copy-start | bytes 7077892
  (42 other events, 173.2 us)
Sparse Core Ops, SparseCore 0:
  89.3 18.0 reduce-scatter.8
  126.3 17.5 reduce-scatter.12
  146.7 13.1 reduce-scatter.10
  180.7 13.1 reduce-scatter.14
  197.9 111.7 reduce-scatter.20
  313.7 57.7 reduce-scatter.18
  376.0 68.0 reduce-scatter.16
  448.6 74.2 reduce-scatter.22
where the time goes:
time: 539 us; the launch traced here: 530 us
  blocking collectives  211 us (39%)
  matrix products  84.1 us (16%)
  waiting for transfers between devices  74 us (14%)
  local copies, waits for them, and re-layouts  69.9 us (13%)
  other arithmetic  66.8 us (12%)
  between operations  16.2 us (3%)
  starting transfers between devices  8.56 us (2%)
    all_gather x1, blocking collectives, shards(): lax.all_gather(d_modulation, ('dp', 'head'), axis=0, tiled=True)  71.3 us
    all_gather x1, blocking collectives, shards(): lax.all_gather(time_cond, ('dp', 'head'), axis=0, tiled=True)  67.7 us
    unnamed x136, local copies, waits for them, and re-layouts  56.4 us
    psum x1, blocking collectives, shards(): lax.psum((pair_weight_grad, pair_gain_grad, d_out_bias), ('dp', 'head'))  37.4 us
    reduce_scatter x1, waiting for transfers between devices, shards(): lax.psum_scatter(down_grad, 'dp', scatter_dimension=1, tiled=True)  29.1 us
    convert_element_type x1, other arithmetic, shards(): norm_back(pair_norm, pair_inv, d_pair_normed * pair_gain)  24.8 us
    dot_general x1, matrix products, shards(): jnp.einsum('chqk,ph->cqkp', d_bias_rows, pair_weight, preferred_element_t...  21.5 us
    reduce_sum x1, other arithmetic, norm_back(): mean_grad = jnp.mean(grad, axis=-1, keepdims=True)  14.5 us
  transfers between devices with their start and end apart: 10, of which 5 were waited for; matrix products, arithmetic and copies ran while one was open for 26% of the time, Pallas kernels for 0%

commit v1 on v0

v1 whole, which is shorter than its diff:
```python
import jax
import jax.numpy as jnp
from jax import lax
from jax.sharding import PartitionSpec as P

DH = 64


epsilon = 1e-05
masked_score = -1000000000.0
precise = lax.Precision.HIGHEST
LANES = 128


def layer_norm(values):
    centred = values - jnp.mean(values, axis=-1, keepdims=True)
    inv_std = lax.rsqrt(jnp.mean(centred * centred, axis=-1, keepdims=True) + epsilon)
    return (centred * inv_std, inv_std)


def norm_back(normed, inv_std, grad):
    mean_grad = jnp.mean(grad, axis=-1, keepdims=True)
    mean_proj = jnp.mean(grad * normed, axis=-1, keepdims=True)
    return inv_std * (grad - mean_grad - normed * mean_proj)


def silu_slope(values):
    sigma = jax.nn.sigmoid(values)
    return sigma * (1.0 + values * (1.0 - sigma))


def head_split(values):
    return values.reshape(values.shape[:-1] + (values.shape[-1] // DH, DH))


def swap_heads(values):
    return lax.ppermute(values, "head", [(0, 1), (1, 0)])


def whole_rows(own, first):
    other = swap_heads(own)
    return jnp.where(
        first,
        jnp.concatenate([own, other], axis=1),
        jnp.concatenate([other, own], axis=1),
    )


def own_rows(values, head, rows):
    return lax.dynamic_slice_in_dim(values, head * rows, rows, 1)


def head_sum(part):
    return part + swap_heads(part)


def attn_scores(queries, keys, biases, valid):
    scores = jnp.einsum("cqhe,ckhe->chqk", queries, keys, preferred_element_type=jnp.float32)
    scores = scores * DH ** (-0.5) + biases.astype(jnp.float32)
    return jnp.where(valid[:, None, None, :], scores, masked_score)


def to_chunks(values, parts):
    return values.reshape(parts, -1, LANES)


def shards(
    layer_input,
    pair_input,
    time_cond,
    chain_lengths,
    residue_mask,
    mod_weight,
    mod_bias,
    qkv_weight,
    pair_gain,
    pair_weight,
    out_weight,
    out_bias,
    gate_up_weight,
    down_weight,
    output_grad,
):
    chains = layer_input.shape[0]
    rows = layer_input.shape[1]
    width = layer_input.shape[2]
    length = residue_mask.shape[1]
    head = lax.axis_index("head")
    first = head == 0
    data_count = lax.axis_size("dp")

    x_rows = whole_rows(layer_input, first)
    g_rows = whole_rows(output_grad, first)

    positions = jnp.arange(length, dtype=jnp.int32)
    valid = (positions[None, :] < chain_lengths[:, None]) & (
        (residue_mask == 1) | (positions[None, :] == 0)
    )
    silu_cond = jax.nn.silu(time_cond).astype(jnp.bfloat16)
    modulation = jnp.dot(silu_cond, mod_weight, preferred_element_type=jnp.float32) + mod_bias
    scale_a, shift_a, gate_a, scale_t, shift_t, gate_t = [
        modulation[:, None, section * width : (section + 1) * width] for section in range(6)
    ]

    pair_norm, pair_inv = layer_norm(pair_input.astype(jnp.float32))
    pair_normed = (pair_norm * pair_gain).astype(jnp.bfloat16)
    bias_rows = jnp.einsum(
        "cqkp,ph->chqk", pair_normed, pair_weight, preferred_element_type=jnp.float32
    ).astype(jnp.bfloat16)
    biases = lax.all_to_all(bias_rows, "head", split_axis=1, concat_axis=2, tiled=True)

    residues = x_rows.astype(jnp.float32)
    norm_in, inv_in = layer_norm(residues)
    normed_a = (norm_in * (1.0 + scale_a) + shift_a).astype(jnp.bfloat16)
    projected = jnp.einsum(
        "cld,dtf->tclf", normed_a, qkv_weight, preferred_element_type=jnp.float32
    ).astype(jnp.bfloat16)
    queries = head_split(projected[0])
    keys = head_split(projected[1])
    values = head_split(projected[2])
    scores = attn_scores(queries, keys, biases, valid)
    row_max = jnp.max(scores, axis=-1, keepdims=True)
    exp_scores = jnp.exp(scores - row_max)
    row_total = jnp.sum(exp_scores, axis=-1, keepdims=True)
    attn_probs = exp_scores / row_total
    probs_low = attn_probs.astype(jnp.bfloat16)
    mixed = jnp.einsum("chqk,ckhe->cqhe", probs_low, values, preferred_element_type=jnp.float32)
    mixed = mixed.reshape(mixed.shape[:2] + (-1,)).astype(jnp.bfloat16)
    attn_part = jnp.einsum("clf,fd->cld", mixed, out_weight, preferred_element_type=jnp.float32)
    attn_branch = head_sum(attn_part) + out_bias
    sig_a = jax.nn.sigmoid(gate_a)
    middle = residues + sig_a * attn_branch

    norm_mid, inv_mid = layer_norm(middle)
    normed_t = (norm_mid * (1.0 + scale_t) + shift_t).astype(jnp.bfloat16)
    gate_up = jnp.einsum(
        "cld,dtf->tclf", normed_t, gate_up_weight, preferred_element_type=jnp.float32
    )
    hidden = (jax.nn.silu(gate_up[0]) * gate_up[1]).astype(jnp.bfloat16)
    ffn_part = jnp.einsum(
        "clf,fd->cld", hidden, down_weight, preferred_element_type=jnp.float32
    ).astype(jnp.bfloat16)
    ffn_branch = ffn_part.astype(jnp.float32) + swap_heads(ffn_part).astype(jnp.float32)
    sig_t = jax.nn.sigmoid(gate_t)
    layer_output = own_rows((middle + sig_t * ffn_branch).astype(jnp.bfloat16), head, rows)

    grad_out = g_rows.astype(jnp.float32)
    d_ffn = (grad_out * sig_t).astype(jnp.bfloat16)
    d_gate_t = jnp.sum(grad_out * ffn_branch * sig_t * (1.0 - sig_t), axis=1)
    down_grad_t = jnp.einsum("cld,clf->df", d_ffn, hidden, preferred_element_type=jnp.float32)
    d_hidden = jnp.einsum("cld,fd->clf", d_ffn, down_weight, preferred_element_type=jnp.float32)
    d_gate = d_hidden * gate_up[1] * silu_slope(gate_up[0])
    d_up = d_hidden * jax.nn.silu(gate_up[0])
    d_gate_up = jnp.stack([d_gate, d_up]).astype(jnp.bfloat16)
    gate_up_grad = jnp.einsum(
        "cld,tclf->dtf", normed_t, d_gate_up, preferred_element_type=jnp.float32
    )
    ffn_in_part = jnp.einsum(
        "tclf,dtf->cld", d_gate_up, gate_up_weight, preferred_element_type=jnp.float32
    )
    d_normed_t = head_sum(ffn_in_part)
    d_middle = grad_out + norm_back(norm_mid, inv_mid, d_normed_t * (1.0 + scale_t))
    d_scale_t = jnp.sum(d_normed_t * norm_mid, axis=1)
    d_shift_t = jnp.sum(d_normed_t, axis=1)
    d_attn = d_middle * sig_a
    d_gate_a = jnp.sum(d_middle * attn_branch * sig_a * (1.0 - sig_a), axis=1)
    d_out_bias = jnp.sum(d_attn, axis=(0, 1))
    d_attn_low = d_attn.astype(jnp.bfloat16)

    out_weight_grad_t = jnp.einsum(
        "cld,clf->df", d_attn_low, mixed, preferred_element_type=jnp.float32
    )
    d_mixed = head_split(
        jnp.einsum(
            "cld,fd->clf", d_attn_low, out_weight, preferred_element_type=jnp.float32
        ).astype(jnp.bfloat16)
    )
    d_values = jnp.einsum("chqk,cqhe->ckhe", probs_low, d_mixed, preferred_element_type=jnp.float32)
    d_probs = jnp.einsum("cqhe,ckhe->chqk", d_mixed, values, preferred_element_type=jnp.float32)
    d_scores = (
        attn_probs * (d_probs - jnp.sum(d_probs * attn_probs, axis=-1, keepdims=True))
    ).astype(jnp.bfloat16)
    d_queries = jnp.einsum(
        "chqk,ckhe->cqhe", d_scores, keys, preferred_element_type=jnp.float32
    ) * DH ** (-0.5)
    d_keys = jnp.einsum(
        "chqk,cqhe->ckhe", d_scores, queries, preferred_element_type=jnp.float32
    ) * DH ** (-0.5)
    d_qkv = (
        jnp.stack([d_queries, d_keys, d_values]).reshape(3, chains, length, -1).astype(jnp.bfloat16)
    )
    qkv_grad = jnp.einsum("cld,tclf->dtf", normed_a, d_qkv, preferred_element_type=jnp.float32)

    packed = jnp.concatenate(
        [
            to_chunks(qkv_grad, data_count),
            to_chunks(out_weight_grad_t, data_count),
            to_chunks(gate_up_grad, data_count),
            to_chunks(down_grad_t, data_count),
        ],
        axis=1,
    ).astype(jnp.bfloat16)
    reduced = lax.psum_scatter(packed, "dp", scatter_dimension=0, tiled=True)[0].astype(
        jnp.float32
    )

    attn_in_part = jnp.einsum(
        "tclf,dtf->cld", d_qkv, qkv_weight, preferred_element_type=jnp.float32
    ).astype(jnp.bfloat16)
    d_normed_a = attn_in_part.astype(jnp.float32) + swap_heads(attn_in_part).astype(jnp.float32)
    input_grad = own_rows(
        d_middle + norm_back(norm_in, inv_in, d_normed_a * (1.0 + scale_a)), head, rows
    )
    d_scale_a = jnp.sum(d_normed_a * norm_in, axis=1)
    d_shift_a = jnp.sum(d_normed_a, axis=1)
    d_modulation = jnp.concatenate(
        [d_scale_a, d_shift_a, d_gate_a, d_scale_t, d_shift_t, d_gate_t], axis=-1
    )

    d_bias_rows = lax.all_to_all(d_scores, "head", split_axis=2, concat_axis=1, tiled=True)
    pair_weight_grad = jnp.einsum(
        "cqkp,chqk->ph", pair_normed, d_bias_rows, preferred_element_type=jnp.float32
    )
    d_pair_normed = jnp.einsum(
        "chqk,ph->cqkp", d_bias_rows, pair_weight, preferred_element_type=jnp.float32
    )
    pair_gain_grad = jnp.sum(d_pair_normed * pair_norm, axis=(0, 1, 2))
    pair_grad = norm_back(pair_norm, pair_inv, d_pair_normed * pair_gain).astype(jnp.bfloat16)

    pair_small = head_sum(
        jnp.concatenate([pair_weight_grad.reshape(-1), pair_gain_grad])[None]
    )
    small = jnp.concatenate(
        [d_modulation, time_cond, pair_small, d_out_bias[None]],
        axis=-1,
    )
    small_rows = lax.all_gather(small, "dp", axis=0, tiled=True)
    mod_size = d_modulation.shape[-1]
    cond_size = time_cond.shape[-1]
    pw_size = pair_weight.size
    pg_size = pair_gain.size
    mod_chain = small_rows[:, :mod_size]
    cond_chain = small_rows[:, mod_size : mod_size + cond_size]
    rest = jnp.sum(small_rows[:, mod_size + cond_size :], axis=0)
    pair_weight_grad = rest[:pw_size].reshape(pair_weight.shape)
    pair_gain_grad = rest[pw_size : pw_size + pg_size]
    out_bias_grad = rest[pw_size + pg_size :]
    cond_act = lax.optimization_barrier(jax.nn.silu(cond_chain).astype(jnp.bfloat16)).astype(
        jnp.float32
    )
    mod_weight_grad = jnp.dot(cond_act.T, mod_chain, precision=precise)
    mod_bias_grad = jnp.sum(mod_chain, axis=0)
    cond_grad = jnp.dot(
        d_modulation, mod_weight.astype(jnp.float32).T, precision=precise
    ) * silu_slope(time_cond)

    sizes = [
        qkv_grad.size // data_count,
        out_weight_grad_t.size // data_count,
        gate_up_grad.size // data_count,
        down_grad_t.size // data_count,
    ]
    flat = reduced.reshape(-1)
    offsets = [0]
    for size in sizes:
        offsets.append(offsets[-1] + size)
    pieces = [flat[offsets[i] : offsets[i + 1]] for i in range(4)]
    qkv_grad = pieces[0].reshape((-1,) + qkv_grad.shape[1:])
    out_weight_grad = pieces[1].reshape(-1, out_weight_grad_t.shape[1]).T
    gate_up_grad = pieces[2].reshape((-1,) + gate_up_grad.shape[1:])
    down_grad = pieces[3].reshape(-1, down_grad_t.shape[1]).T
    return (
        layer_output,
        input_grad,
        pair_grad,
        cond_grad,
        mod_weight_grad,
        mod_bias_grad,
        qkv_grad,
        pair_gain_grad,
        pair_weight_grad,
        out_weight_grad,
        out_bias_grad,
        gate_up_grad,
        down_grad,
    )


def solution(mesh):
    placed = (
        P("dp", "head", None),
        P("dp", "head", None, None),
        P("dp", None),
        P("dp"),
        P("dp", None),
        P(),
        P(),
        P(None, None, "head"),
        P(),
        P(),
        P("head", None),
        P(),
        P(None, None, "head"),
        P("head", None),
        P("dp", "head", None),
    )
    return jax.shard_map(
        shards,
        mesh=mesh,
        in_specs=placed,
        out_specs=(
            P("dp", "head", None),
            P("dp", "head", None),
            P("dp", "head", None, None),
            P("dp", None),
            P(),
            P(),
            P("dp", None, "head"),
            P(),
            P(),
            P("head", "dp"),
            P(),
            P("dp", None, "head"),
            P("head", "dp"),
        ),
        check_vma=False,
    )
```

time: 539 us -> 382 us (0.71)
  blocking collectives: 211 us -> 23.6 us
  local copies, waits for them, and re-layouts: 69.9 us -> 121 us
  waiting for transfers between devices: 74 us -> 33 us
  other arithmetic: 66.8 us -> 77.6 us
  starting transfers between devices: 8.56 us -> 17.2 us
    all_gather x6 -> x1, blocking collectives: 173 us -> 23.6 us  [shards(): small_rows = lax.all_gather(small, 'dp', axis=0, tiled=True)]
    reduce_scatter x8 -> x1, waiting for transfers between devices: 68.4 us -> 0.01 us  [shards(): lax.psum_scatter(packed, 'dp', scatter_dimension=0, tiled=True)[0]]
    psum x1 -> x0, blocking collectives: 37.4 us -> none  [shards(): lax.psum((pair_weight_grad, pair_gain_grad, d_out_bias), ('dp', 'head'))]
    reshape x1 -> x10, local copies, waits for them, and re-layouts: 0.34 us -> 28 us  [the longest x4 25.1 us: to_chunks(): return values.reshape(parts, -1, LANES)]
    ppermute x0 -> x7, waiting for transfers between devices: none -> 26.1 us  [swap_heads(): return lax.ppermute(values, 'head', [(0, 1), (1, 0)])]
    another operation x0 -> x2, local copies, waits for them, and re-layouts: none -> 12.2 us
    slice x5 -> x11, local copies, waits for them, and re-layouts: 0.51 us -> 10.1 us  [the longest x4 2.93 us: shards(): pieces = [flat[offsets[i]:offsets[i + 1]] for i in range(4)]]
    ppermute x0 -> x7, starting transfers between devices: none -> 9.61 us  [swap_heads(): return lax.ppermute(values, 'head', [(0, 1), (1, 0)])]
  transfers between devices with their start and end apart: 10 -> 10, of which waited for: 5 -> 3; matrix products, arithmetic and copies ran while one was open for 26% -> 56% of each run, Pallas kernels for 0% -> 0%
where the time goes in v1:
time: 382 us; the launch traced here: 375 us
  local copies, waits for them, and re-layouts  121 us (32%)
  matrix products  87 us (23%)
  other arithmetic  77.6 us (20%)
  waiting for transfers between devices  33 us (9%)
  blocking collectives  23.6 us (6%)
  starting transfers between devices  17.2 us (5%)
  between operations  15.8 us (4%)
    unnamed x144, local copies, waits for them, and re-layouts  52.1 us
    ppermute x7, waiting for transfers between devices, swap_heads(): return lax.ppermute(values, 'head', [(0, 1), (1, 0)])  26.1 us
    reshape x4, local copies, waits for them, and re-layouts, to_chunks(): return values.reshape(parts, -1, LANES)  25.1 us
    convert_element_type x1, other arithmetic, shards(): norm_back(pair_norm, pair_inv, d_pair_normed * pair_gain)  24.9 us
    all_gather x1, blocking collectives, shards(): small_rows = lax.all_gather(small, 'dp', axis=0, tiled=True)  23.6 us
    dot_general x1, matrix products, shards(): jnp.einsum('chqk,ph->cqkp', d_bias_rows, pair_weight, preferred_element_t...  21.5 us
    reduce_sum x1, other arithmetic, norm_back(): mean_grad = jnp.mean(grad, axis=-1, keepdims=True)  15.2 us
    another operation x2, local copies, waits for them, and re-layouts  12.2 us
  transfers between devices with their start and end apart: 10, of which 3 were waited for; matrix products, arithmetic and copies ran while one was open for 56% of the time, Pallas kernels for 0%

profile of v1, /device:TPU:0, one launch (start us, length us, event | category | flops | bytes accessed | tf_op | source)
XLA Modules:
  0.0 375.2 jit_solution(14148207465790848436)
XLA Ops:
  7.2 3.0 collective-permute-start
  10.2 22.4 %copy.116 = bf16[1,128,256,256]{2,3,1,0:T(8,128)(2,1)} copy(bf16[1,128,256,256]{3,2,1,0:T(8,128)(2,1)} %param.16) | data formatting | bytes 33554432 | tf_op args[1]
  32.6 6.9 %convert_reduce_fusion = f32[128,256]{1,0:T(8,128)S(1)} fusion(bf16[1,128,256,256]{2,3,1,0:T(8,128)(2,1)} %copy.116), kind=kLoop, calls=%fused_computation.2 | loop fusion | flops 16744448 | bytes 16908288 | tf_op jit(solution)/shard_map/reduce_sum | solution.py:16
  39.5 3.7 copy-done.2
  43.3 4.7 %fusion.13 = f32[128,256]{1,0:T(8,128)S(1)} fusion(bf16[1,128,256,256]{2,3,1,0:T(8,128)(2,1)S(1)} %copy-done.2, f32[128,256]{1,0:T(8,128)S(1)} %broadcast_multiply_fusion.2), kind=kLoop, calls=%fused_computation.15 | loop fusion | flops 33521664 | bytes 17039360 | tf_op jit(solution)/shard_map/reduce_sum | solution.py:17
  48.0 5.2 %fusion.39 = bf16[1,12,128,256]{3,1,2,0:T(8,128)(2,1)S(1)} fusion(bf16[1,128,256,256]{2,3,1,0:T(8,128)(2,1)S(1)} %copy-done.2, f32[256]{0:T(256)S(1)} %copy-done.52, f32[128,256]{1,0:T(8,128)S(1)} %add_rsqrt_fusion, f32[128,256]{1,0:T(8,128)S(1)} %broadcast_multiply_fusion.2, bf16[256,12]{0,1:T(8,128)(2,1)S(1)} %copy-done.61), kind=kOutput, calls=%fused_computation.52 | convolution fusion | flops 243662848 | bytes 17832960 | tf_op jit(solution)/shard_map/cqkp,ph->chqk/dot_general | solution.py:107
  54.4 3.7 all-to-all-start
  73.3 3.7 copy.120
  76.9 3.4 reshape.1017
  84.8 3.1 convolution_convert_fusion.8
  92.2 17.9 %collective-permute-done.1 = f32[1,256,768]{2,1,0:T(8,128)} collective-permute-done((f32[1,256,768]{2,1,0:T(8,128)S(1)}, f32[1,256,768]{2,1,0:T(8,128)}, u32[]{:S(2)}, u32[]{:S(2)}) %collective-permute-start.1) | collective-permute-done | bytes 786464 | tf_op jit(solution)/shard_map/ppermute | solution.py:37
  112.0 4.0 %fusion.19 = f32[2,1,256,1536]{3,2,0,1:T(8,128)S(1)} fusion(bf16[768,2,1536]{2,1,0:T(2,128)(2,1)} %param.27, f32[1,256,768]{2,1,0:T(8,128)S(1)} %get-tuple-element.87, f32[768]{0:T(1024)} %get-tuple-element.78, f32[768]{0:T(1024)S(1)} %get-tuple-element.79, f32[256]{0:T(256)S(1)} %add_rsqrt_fusion.1, f32[256]{0:T(256)S(1)} %broadcast_multiply_fusion.7), kind=kOutput, calls=%fused_computation.25 | convolution fusion | flops 1208942592 | bytes 8658944 | tf_op jit(solution)/shard_map/cld,dtf->tclf/dot_general | solution.py:136
  123.1 3.4 convolution_convert_fusion.1
  126.5 5.8 %reshape.1011 = bf16[16,576,128]{2,1,0:T(8,128)(2,1)} reshape(bf16[768,1536]{1,0:T(8,128)(2,1)} %convolution_convert_fusion.1) | data formatting | bytes 4718592 | tf_op jit(solution)/shard_map/reshape | solution.py:64
  132.3 5.1 %convolution_convert_fusion = bf16[768,2,1536]{2,0,1:T(8,128)(2,1)} fusion(bf16[1,256,1536]{2,1,0:T(8,128)(2,1)} %copy-done.23, bf16[1,256,1536]{2,1,0:T(8,128)(2,1)} %copy-done.22, f32[1,256,768]{2,1,0:T(8,128)S(1)} %get-tuple-element.87, f32[768]{0:T(1024)} %get-tuple-element.78, f32[768]{0:T(1024)S(1)} %get-tuple-element.79, f32[256]{0:T(256)} %copy-done.46, ...), kind=kOutput, calls=%fused_computation.19 | convolution fusion | flops 1214447616 | bytes 7086080 | tf_op jit(solution)/shard_map/cld,tclf->dtf/dot_general | solution.py:155
  137.5 9.3 %copy.141 = bf16[768,2,1536]{2,1,0:T(2,128)(2,1)} copy(bf16[768,2,1536]{2,0,1:T(8,128)(2,1)} %convolution_convert_fusion) | data formatting | bytes 9437184 | tf_op jit(solution)/shard_map/convert.10
  146.8 11.4 %reshape.1010 = bf16[16,1152,128]{2,1,0:T(8,128)(2,1)} reshape(bf16[768,2,1536]{2,1,0:T(2,128)(2,1)} %copy.141) | data formatting | bytes 9437184 | tf_op jit(solution)/shard_map/reshape | solution.py:64
  167.4 3.2 convolution_convert_fusion.6
  185.4 2.9 copy.139
  188.3 5.4 %reshape.1008 = bf16[16,432,128]{2,1,0:T(8,128)(2,1)} reshape(bf16[768,3,384]{2,1,0:T(4,128)(2,1)} %copy.139) | data formatting | bytes 3538944 | tf_op jit(solution)/shard_map/reshape | solution.py:64
  193.7 7.5 %pad_maximum_fusion = bf16[16,2304,128]{2,1,0:T(8,128)(2,1)} fusion(bf16[16,576,128]{2,1,0:T(8,128)(2,1)} %reshape.1011, bf16[16,1152,128]{2,1,0:T(8,128)(2,1)} %reshape.1010, bf16[16,144,128]{2,1,0:T(8,128)(2,1)} %reshape.1009, bf16[16,432,128]{2,1,0:T(8,128)(2,1)} %reshape.1008), kind=kLoop, calls=%fused_computation.18 | loop fusion | flops 37748736 | bytes 18874368 | tf_op jit(solution)/shard_map/concatenate | solution.py:194
  201.2 3.0 fusion.48
  207.7 8.2 %collective-permute-done.2 = bf16[1,256,768]{2,1,0:T(8,128)(2,1)S(1)} collective-permute-done((bf16[1,256,768]{2,1,0:T(8,128)(2,1)S(1)}, bf16[1,256,768]{2,1,0:T(8,128)(2,1)S(1)}, u32[]{:S(2)}, u32[]{:S(2)}) %collective-permute-start.2) | collective-permute-done | bytes 393248 | tf_op jit(solution)/shard_map/ppermute | solution.py:37
  219.8 3.7 all-to-all-start.1
  226.1 6.8 %all-to-all-done.1 = bf16[1,6,256,256]{3,1,0,2:T(8,128)(2,1)S(1)} async-done(((bf16[1,6,256,256]{3,1,0,2:T(8,128)(2,1)}), bf16[1,6,256,256]{3,1,0,2:T(8,128)(2,1)S(1)}, u32[]{:S(2)}, u32[]{:S(2)}) %all-to-all-start.1) | async-done | bytes 786464 | tf_op jit(solution)/shard_map/all_to_all | solution.py:220
  233.1 10.0 %fusion.51 = f32[256,12]{1,0:T(8,128)S(1)} fusion(bf16[1,128,256,256]{2,3,1,0:T(8,128)(2,1)} %copy.116, f32[256]{0:T(256)S(1)} %copy-done.53, f32[128,256]{1,0:T(8,128)S(1)} %copy-done.29, f32[128,256]{1,0:T(8,128)S(1)} %copy-done.21, bf16[12,128,256]{2,1,0:T(8,128)(2,1)S(1)} %bitcast.217), kind=kOutput, calls=%fused_computation.73 | convolution fusion | flops 243269632 | bytes 17839104 | tf_op jit(solution)/shard_map/cqkp,chqk->ph/dot_general | solution.py:221
  243.3 21.5 %fusion.12 = (f32[256]{0:T(256)S(1)}, f32[128,256]{1,0:T(8,128)S(1)}, f32[128,256,256]{1,2,0:T(8,128)}) fusion(bf16[1,128,256,256]{2,3,1,0:T(8,128)(2,1)} %copy.116, f32[128,256]{1,0:T(8,128)S(1)} %copy-done.29, f32[128,256]{1,0:T(8,128)S(1)} %copy-done.21, f32[256]{0:T(256)S(1)} %copy-done.53, bf16[256,12]{0,1:T(8,128)(2,1)S(1)} %copy-done.62, ...), kind=kOutput, calls=%fused_computation.14 | convolution fusion | flops 268402432 | bytes 51519488 | tf_op jit(solution)/shard_map/chqk,ph->cqkp/dot_general | solution.py:224
  265.3 15.2 %multiply_reduce_fusion = f32[128,256]{1,0:T(8,128)S(1)} fusion(f32[128,256,256]{1,2,0:T(8,128)} %get-tuple-element.115, f32[256]{0:T(256)S(1)} %copy-done.53), kind=kLoop, calls=%fused_computation.16 | loop fusion | flops 16744448 | bytes 33686528 | tf_op jit(solution)/shard_map/reduce_sum | solution.py:22
  284.0 24.9 %fusion.11 = bf16[1,128,256,256]{2,3,1,0:T(8,128)(2,1)} fusion(bf16[1,128,256,256]{2,3,1,0:T(8,128)(2,1)} %copy.116, f32[128,256,256]{1,2,0:T(8,128)} %get-tuple-element.115, f32[128,256]{1,0:T(8,128)S(1)} %broadcast_multiply_fusion, f32[128,256]{1,0:T(8,128)S(1)} %broadcast_multiply_fusion.1, f32[256]{0:T(256)S(1)} %copy-done.53, ...), kind=kLoop, calls=%fused_computation.13 | loop fusion | flops 75497472 | bytes 67634176 | tf_op jit(solution)/shard_map/convert_element_type | solution.py:228
  308.8 22.4 %copy.142 = bf16[1,128,256,256]{3,2,1,0:T(8,128)(2,1)} copy(bf16[1,128,256,256]{2,3,1,0:T(8,128)(2,1)} %fusion.11) | data formatting | bytes 33554432
  331.3 23.6 %all-gather = f32[16,1,8960]{2,1,0:T(1,128)S(1)} all-gather(f32[1,1,8960]{2,1,0:T(1,128)S(1)} %bitcast.228), channel_id=1, replica_groups=mesh['dp'=16,'head'=2] {'dp'}, dimensions={0}, use_global_device_ids=true | all-gather | bytes 609280 | tf_op jit(solution)/shard_map/all_gather | solution.py:237
  357.6 4.2 %fusion.77 = f32[256,4608]{1,0:T(8,128)} fusion(bf16[16,256]{1,0:T(8,128)(2,1)S(1)} %multiply_convert_fusion.8, f32[16,8960]{1,0:T(8,128)S(1)} %bitcast.202), kind=kOutput, calls=%fused_computation.129 | convolution fusion | flops 226492416 | bytes 5021696 | tf_op jit(solution)/shard_map/dot_general | solution.py:251
  (237 shorter events, 80.4 us)
Async XLA Ops:
  7.2 108.9 %copy-start = (bf16[1536,768]{1,0:T(8,128)(2,1)S(1)}, bf16[1536,768]{1,0:T(8,128)(2,1)}, u32[]{:S(2)}) copy-start(bf16[1536,768]{1,0:T(8,128)(2,1)} %param.28) | copy-start | bytes 7077892
  7.2 56.0 %collective-permute-start = (bf16[1,128,768]{2,1,0:T(8,128)(2,1)}, bf16[1,128,768]{2,1,0:T(8,128)(2,1)S(1)}, u32[]{:S(2)}, u32[]{:S(2)}) collective-permute-start(bf16[1,128,768]{2,1,0:T(8,128)(2,1)} %param.15), channel_id=1, source_target_pairs={{0,1},{1,0},{2,3},{3,2},{4,5},{5,4},{6,7},{7,6},{8,9},{9,8},{10,11... | collective-permute-start | bytes 589832 | tf_op jit(solution)/shard_map/ppermute | solution.py:37
  32.6 10.7 %copy-start.2 = (bf16[1,128,256,256]{2,3,1,0:T(8,128)(2,1)S(1)}, bf16[1,128,256,256]{2,3,1,0:T(8,128)(2,1)}, u32[]{:S(2)}) copy-start(bf16[1,128,256,256]{2,3,1,0:T(8,128)(2,1)} %copy.116) | copy-start | bytes 50331652
  54.4 7.4 %copy-start.58 = (s32[1,256]{1,0:T(1,128)S(1)}, s32[1,256]{1,0:T(1,128)}, u32[]{:S(2)}) copy-start(s32[1,256]{1,0:T(1,128)} %param.19) | copy-start | bytes 3076
  54.4 8.8 %copy-start.12 = (bf16[1,128,768]{2,1,0:T(8,128)(2,1)S(1)}, bf16[1,128,768]{2,1,0:T(8,128)(2,1)}, u32[]{:S(2)}) copy-start(bf16[1,128,768]{2,1,0:T(8,128)(2,1)} %param.15) | copy-start | bytes 589828
  54.4 17.6 %all-to-all-start = ((bf16[1,12,128,256]{3,2,0,1:T(8,128)(2,1)}), bf16[1,12,128,256]{3,2,0,1:T(8,128)(2,1)S(1)}, u32[]{:S(2)}, u32[]{:S(2)}) async-start(bf16[1,12,128,256]{3,2,0,1:T(8,128)(2,1)} %copy.118), calls=%async_computation | async-start | bytes 1572864 | tf_op jit(solution)/shard_map/all_to_all | solution.py:110
  58.0 303.8 %reduce-scatter.2.cloned.1.call-start = ((), (), s32[]{:S(2)}) async-start(), calls=%async_computation.3 | async-start | bytes 10027008 | tf_op jit(solution)/shard_map/reduce_scatter | solution.py:203
  84.8 25.3 %copy-start.41 = (f32[768]{0:T(1024)S(1)}, f32[768]{0:T(1024)}, u32[]{:S(2)}) copy-start(f32[768]{0:T(1024)} %param.26) | copy-start | bytes 9220
  89.5 20.6 %collective-permute-start.1 = (f32[1,256,768]{2,1,0:T(8,128)S(1)}, f32[1,256,768]{2,1,0:T(8,128)}, u32[]{:S(2)}, u32[]{:S(2)}) collective-permute-start(f32[1,256,768]{2,1,0:T(8,128)S(1)} %convolution_bitcast_fusion), channel_id=1, source_target_pairs={{0,1},{1,0},{2,3},{3,2},{4,5},{5,4},{6,7},{7,6},{8,9},{9,8},{10,11... | collective-permute-start | bytes 2359304 | tf_op jit(solution)/shard_map/ppermute | solution.py:37
  91.5 24.5 %collective-permute-start.3 = (bf16[1,128,768]{2,1,0:T(8,128)(2,1)}, bf16[1,128,768]{2,1,0:T(8,128)(2,1)}, u32[]{:S(2)}, u32[]{:S(2)}) collective-permute-start(bf16[1,128,768]{2,1,0:T(8,128)(2,1)} %param.29), channel_id=1, source_target_pairs={{0,1},{1,0},{2,3},{3,2},{4,5},{5,4},{6,7},{7,6},{8,9},{9,8},{10,11... | collective-permute-start | bytes 589832 | tf_op jit(solution)/shard_map/ppermute | solution.py:37
  121.2 37.1 %collective-permute-start.4 = (f32[1,256,768]{2,1,0:T(8,128)}, f32[1,256,768]{2,1,0:T(8,128)}, u32[]{:S(2)}, u32[]{:S(2)}) collective-permute-start(f32[1,256,768]{2,1,0:T(8,128)} %fusion.42), channel_id=1, source_target_pairs={{0,1},{1,0},{2,3},{3,2},{4,5},{5,4},{6,7},{7,6},{8,9},{9,8},{10,11... | collective-permute-start | bytes 2359304 | tf_op jit(solution)/shard_map/ppermute | solution.py:37
  173.6 9.8 %copy-start.40 = (f32[768]{0:T(1024)S(1)}, f32[768]{0:T(1024)}, u32[]{:S(2)}) copy-start(f32[768]{0:T(1024)} %copy-done.39) | copy-start | bytes 9220
  173.6 9.8 %copy-start.51 = (f32[256]{0:T(256)S(1)}, f32[256]{0:T(256)}, u32[]{:S(2)}) copy-start(f32[256]{0:T(256)} %copy-done.50) | copy-start | bytes 3076
  173.6 9.8 %copy-start.55 = (f32[256]{0:T(256)S(1)}, f32[256]{0:T(256)}, u32[]{:S(2)}) copy-start(f32[256]{0:T(256)} %copy-done.54) | copy-start | bytes 3076
  204.2 11.7 %copy-start.27 = (bf16[1,128,768]{2,1,0:T(8,128)(2,1)S(1)}, bf16[1,128,768]{2,1,0:T(8,128)(2,1)}, u32[]{:S(2)}) copy-start(bf16[1,128,768]{2,1,0:T(8,128)(2,1)} %param.29) | copy-start | bytes 589828
  204.2 11.7 %collective-permute-start.2 = (bf16[1,256,768]{2,1,0:T(8,128)(2,1)S(1)}, bf16[1,256,768]{2,1,0:T(8,128)(2,1)S(1)}, u32[]{:S(2)}, u32[]{:S(2)}) collective-permute-start(bf16[1,256,768]{2,1,0:T(8,128)(2,1)S(1)} %fusion.48), channel_id=1, source_target_pairs={{0,1},{1,0},{2,3},{3,2},{4,5},{5,4},{6,7},{7,6},{8,9},{9,8},{10,11... | collective-permute-start | bytes 1179656 | tf_op jit(solution)/shard_map/ppermute | solution.py:37
  205.7 12.4 %copy-start.4 = (bf16[6,256,256]{1,2,0:T(8,128)(2,1)S(1)}, bf16[6,256,256]{1,2,0:T(8,128)(2,1)}, u32[]{:S(2)}) copy-start(bf16[6,256,256]{1,2,0:T(8,128)(2,1)} %copy-done.3) | copy-start | bytes 2359300
  205.7 17.8 %collective-permute-start.5 = (bf16[1,256,768]{2,1,0:T(8,128)(2,1)S(1)}, bf16[1,256,768]{2,1,0:T(8,128)(2,1)}, u32[]{:S(2)}, u32[]{:S(2)}) collective-permute-start(bf16[1,256,768]{2,1,0:T(8,128)(2,1)S(1)} %fusion.47), channel_id=1, source_target_pairs={{0,1},{1,0},{2,3},{3,2},{4,5},{5,4},{6,7},{7,6},{8,9},{9,8},{10,11... | collective-permute-start | bytes 1179656 | tf_op jit(solution)/shard_map/ppermute | solution.py:37
  219.8 13.0 %all-to-all-start.1 = ((bf16[1,6,256,256]{3,1,0,2:T(8,128)(2,1)}), bf16[1,6,256,256]{3,1,0,2:T(8,128)(2,1)S(1)}, u32[]{:S(2)}, u32[]{:S(2)}) async-start(bf16[1,6,256,256]{3,1,0,2:T(8,128)(2,1)} %copy.131), calls=%async_computation.1 | async-start | bytes 2097152 | tf_op jit(solution)/shard_map/all_to_all | solution.py:220
  225.9 7.2 %copy-start.29 = (f32[128,256]{1,0:T(8,128)S(1)}, f32[128,256]{1,0:T(8,128)}, u32[]{:S(2)}) copy-start(f32[128,256]{1,0:T(8,128)} %copy-done.28) | copy-start | bytes 393220
  225.9 7.2 %copy-start.53 = (f32[256]{0:T(256)S(1)}, f32[256]{0:T(256)}, u32[]{:S(2)}) copy-start(f32[256]{0:T(256)} %param.23) | copy-start | bytes 3076
  233.1 10.1 %copy-start.62 = (bf16[256,12]{0,1:T(8,128)(2,1)S(1)}, bf16[256,12]{0,1:T(8,128)(2,1)}, u32[]{:S(2)}) copy-start(bf16[256,12]{0,1:T(8,128)(2,1)} %param.24) | copy-start | bytes 18436
  243.2 21.9 %copy-start.44 = (f32[768]{0:T(1024)S(1)}, f32[768]{0:T(1024)}, u32[]{:S(2)}) copy-start(f32[768]{0:T(1024)} %get-tuple-element.71) | copy-start | bytes 9220
  243.3 22.0 %copy-start.38 = (f32[768]{0:T(1024)S(1)}, f32[768]{0:T(1024)}, u32[]{:S(2)}) copy-start(f32[768]{0:T(1024)} %get-tuple-element.67) | copy-start | bytes 9220
  243.3 22.0 %copy-start.37 = (f32[768]{0:T(1024)S(1)}, f32[768]{0:T(1024)}, u32[]{:S(2)}) copy-start(f32[768]{0:T(1024)} %get-tuple-element.72) | copy-start | bytes 9220
  264.8 66.4 %collective-permute-start.6 = (f32[1,3328]{1,0:T(1,128)S(1)}, f32[1,3328]{1,0:T(1,128)S(1)}, u32[]{:S(2)}, u32[]{:S(2)}) collective-permute-start(f32[1,3328]{1,0:T(1,128)S(1)} %broadcast_in_dim.17), channel_id=1, source_target_pairs={{0,1},{1,0},{2,3},{3,2},{4,5},{5,4},{6,7},{7,6},{8,9},{9,8},{10,11... | collective-permute-start | bytes 39944 | tf_op jit(solution)/shard_map/ppermute | solution.py:37
  265.3 15.2 %copy-start.6 = (f32[1,256,768]{2,1,0:T(8,128)S(1)}, f32[1,256,768]{2,1,0:T(8,128)}, u32[]{:S(2)}) copy-start(f32[1,256,768]{2,1,0:T(8,128)} %copy-done.5) | copy-start | bytes 2359300
  265.3 15.2 %copy-start.15 = (f32[1,256,768]{2,1,0:T(8,128)S(1)}, f32[1,256,768]{2,1,0:T(8,128)}, u32[]{:S(2)}) copy-start(f32[1,256,768]{2,1,0:T(8,128)} %get-tuple-element.98) | copy-start | bytes 2359300
  265.3 15.2 %copy-start.59 = (f32[128]{0:T(128)S(1)}, f32[128]{0:T(128)}, u32[]{:S(2)}) copy-start(f32[128]{0:T(128)} %dynamic-slice.2) | copy-start | bytes 1540
  265.3 16.1 %copy-start.7 = (bf16[256,4608]{1,0:T(8,128)(2,1)S(1)}, bf16[256,4608]{1,0:T(8,128)(2,1)}, u32[]{:S(2)}) copy-start(bf16[256,4608]{1,0:T(8,128)(2,1)} %param.20) | copy-start | bytes 7077892
  265.3 16.1 %copy-start.49 = (f32[1,256]{1,0:T(1,128)S(1)}, f32[1,256]{1,0:T(1,128)}, u32[]{:S(2)}) copy-start(f32[1,256]{1,0:T(1,128)} %param.17) | copy-start | bytes 3076
  308.8 22.4 %copy-start.43 = (f32[768]{0:T(1024)S(1)}, f32[768]{0:T(1024)}, u32[]{:S(2)}) copy-start(f32[768]{0:T(1024)} %get-tuple-element.70) | copy-start | bytes 9220
  (44 other events, 153.0 us)
Sparse Core Ops, SparseCore 0:
  201.3 111.5 reduce-scatter.1
